TPU v7x, 512 devices: a whole 4x4x16 slice. The times are simulated.
512 devices in a mesh: ingest: 8 (over y, core), owner: 64 (over x, z).
Axes of the slice: x: 4, y: 4, z: 16, core: 2. Of those that a mesh axis runs over, the one named last changes fastest.
Arguments:
- frame_rows: bfloat16 [2112, 28, 1024], P('owner', None, 'ingest'), may hold values from -32 to 32
- route_owner: int32 [2112], P('owner'), may hold values from 0 to 63, as said below
- route_slot: int32 [2112], P('owner'), may hold values from 0 to 32, as said below
- frames: int32 [2112], P('owner'), may hold values from 1 to 28, as said below
- kv_cache: bfloat16 [2112, 8, 70, 256], P('owner', 'ingest'), may hold values from -250 to 250
- conv_cache: bfloat16 [2112, 8, 1024], P('owner', None, 'ingest'), may hold values from -5 to 5
- mig_owner: int32 [2048], P('owner'), may hold values from 0 to 63, as said below
- ln1_gain: float32 [1024], replicated, may hold values from 0.1 to 1.9
- w_qkv: bfloat16 [1024, 8, 384], P(None, 'ingest'), may hold values from -0.1875 to 0.1875
- w_out: bfloat16 [1024, 1024], P('ingest'), may hold values from -0.1875 to 0.1875
- ln2_gain: float32 [1024], replicated, may hold values from 0.1 to 1.9
- w_pw1: bfloat16 [1024, 2, 1024], P(None, None, 'ingest'), may hold values from -0.1875 to 0.1875
- dw_weight: bfloat16 [9, 1024], P(None, 'ingest'), may hold values from -2 to 2
- bn_scale: float32 [1024], P('ingest'), may hold values from 0.1 to 1.9
- bn_shift: float32 [1024], P('ingest'), may hold values from -2.5 to 2.5
- w_pw2: bfloat16 [1024, 1024], P('ingest'), may hold values from -0.1875 to 0.1875
Outputs:
- layer_out: bfloat16 [2112, 28, 1024], P('owner', None, 'ingest')
- kv_next: bfloat16 [2112, 8, 70, 256], P('owner', 'ingest')
- conv_next: bfloat16 [2112, 8, 1024], P('owner', None, 'ingest')
Inputs may be any that keep to these rules, and one draw needn't show every extreme that they name: `route_owner`: every owner receives exactly 33 utterances. The utterances that one source device along owner (a block of 33 rows in arrival order) sends to one owner number at most 1, and some source device reaches that number. `route_slot`: the utterances sent to one owner have distinct slots. Every owner holds an utterance with 28 new frames. The utterance in old slot 1 + j of an owner moves to slot 1 + j of owner mig_owner; the 32 utterances of one owner go to 32 different other owners, and every owner receives exactly one utterance for each j.
All inputs are finite; a program needn't handle non-finite values.
Results may differ from a plain program's by a relative error of at most 0.01.
Values may be sent and summed in bfloat16 or wider, within the bound.
No kernel may reach another device: no remote copies, remote signals or barrier semaphores. Data moves between devices by JAX's collectives and lax.ppermute only.
A program may use at most 64 MiB of HBM per device.

v0:
```python
import jax
import jax.numpy as jnp
from jax import lax
from jax.sharding import PartitionSpec as P

BLOCKS = 2
norm_eps = 1e-05


def normalize(values, gain_cols):
    model_width = values.shape[-1]
    row_mean = jnp.sum(values, axis=-1, keepdims=True) / model_width
    spread = jnp.sum(values * values, axis=-1, keepdims=True) / model_width - row_mean * row_mean
    return ((values - row_mean) * lax.rsqrt(spread + norm_eps) * gain_cols).astype(jnp.bfloat16)


def shards(
    frame_rows,
    route_owner,
    route_slot,
    frames,
    kv_cache,
    conv_cache,
    mig_owner,
    ln1_gain,
    w_qkv,
    w_out,
    ln2_gain,
    w_pw1,
    dw_weight,
    bn_scale,
    bn_shift,
    w_pw2,
):
    owners = lax.axis_size("owner")
    groups = lax.axis_size("ingest")
    me = lax.axis_index("ingest")
    utterances, frame_span, local_width = frame_rows.shape
    model_width = w_qkv.shape[0]
    head_dim = w_qkv.shape[2] // 3
    cache_len = kv_cache.shape[2]
    conv_len = conv_cache.shape[1]
    taps = dw_weight.shape[0]
    horizon = frame_span // BLOCKS
    moving = mig_owner.shape[0]
    settled = utterances - moving
    dest = jnp.arange(owners, dtype=jnp.int32)
    frame_pad = -(-(frame_span + 1) // 16) * 16
    slot_tag = jnp.broadcast_to(
        (route_slot + 1).astype(jnp.bfloat16)[:, None, None], (utterances, 1, local_width)
    )
    frame_rows_tagged = jnp.concatenate(
        [
            frame_rows,
            slot_tag,
            jnp.zeros((utterances, frame_pad - frame_span - 1, local_width), jnp.bfloat16),
        ],
        axis=1,
    )
    frame_send = jnp.einsum(
        "ds,stc->dtc",
        (dest[:, None] == route_owner[None, :]).astype(jnp.bfloat16),
        frame_rows_tagged,
        preferred_element_type=jnp.float32,
    ).astype(jnp.bfloat16)
    frame_got = lax.all_to_all(frame_send, "owner", split_axis=0, concat_axis=0, tiled=True)
    kv_lanes = 2 * head_dim
    conv_fold = conv_len * local_width // kv_lanes
    cache_used = cache_len + conv_fold + 1
    cache_pad = -(-cache_used // 16) * 16
    mover_tag = jnp.broadcast_to(
        (jnp.arange(moving, dtype=jnp.int32) + 1).astype(jnp.bfloat16)[:, None, None],
        (moving, 1, kv_lanes),
    )
    cache_rows = jnp.concatenate(
        [
            kv_cache[settled:, 0],
            conv_cache[settled:].reshape(moving, conv_fold, kv_lanes),
            mover_tag,
            jnp.zeros((moving, cache_pad - cache_used, kv_lanes), jnp.bfloat16),
        ],
        axis=1,
    )
    cache_send = jnp.einsum(
        "dj,jrc->drc",
        (dest[:, None] == mig_owner[None, :]).astype(jnp.bfloat16),
        cache_rows,
        preferred_element_type=jnp.float32,
    ).astype(jnp.bfloat16)
    cache_got = lax.all_to_all(cache_send, "owner", split_axis=0, concat_axis=0, tiled=True)
    got_slot = frame_got[:, frame_span, 0].astype(jnp.int32)
    slots = jnp.arange(utterances, dtype=jnp.int32)
    arranged = jnp.einsum(
        "so,otc->stc",
        (slots[:, None] + 1 == got_slot[None, :]).astype(jnp.bfloat16),
        frame_got[:, :frame_span],
        preferred_element_type=jnp.float32,
    ).astype(jnp.bfloat16)
    out_span = frame_span
    frame_span = -(-frame_span // 16) * 16
    arranged = jnp.pad(arranged, ((0, 0), (0, frame_span - out_span), (0, 0)))
    x_all = lax.all_gather(arranged, "ingest", axis=0, tiled=False)
    w_out_in, w_pw2_in, x_all = lax.optimization_barrier((w_out, w_pw2, x_all))
    w_out_full = lax.all_gather(w_out_in, "ingest", axis=0, tiled=True)
    w_pw2_full = lax.all_gather(w_pw2_in, "ingest", axis=0, tiled=True)
    x_plain = x_all.transpose(1, 2, 0, 3).reshape(utterances, frame_span, model_width)
    normed = normalize(x_plain.astype(jnp.float32), ln1_gain)
    projected = jnp.dot(
        normed, w_qkv.reshape(model_width, 3 * head_dim), preferred_element_type=jnp.float32
    )
    queries = projected[..., :head_dim].astype(jnp.bfloat16)
    fresh = projected[..., head_dim:].astype(jnp.bfloat16)
    w_out_full, w_pw2_full, x_plain, queries, fresh = lax.optimization_barrier(
        (w_out_full, w_pw2_full, x_plain, queries, fresh)
    )
    w_pw2_cols = lax.dynamic_slice_in_dim(w_pw2_full, me * local_width, local_width, 1).reshape(
        groups, local_width, local_width
    )
    got_mover = cache_got[:, cache_used - 1, 0].astype(jnp.int32)
    movers = jnp.arange(moving, dtype=jnp.int32)
    moved = jnp.einsum(
        "jo,orc->jrc",
        (movers[:, None] + 1 == got_mover[None, :]).astype(jnp.bfloat16),
        cache_got[:, : cache_used - 1],
        preferred_element_type=jnp.float32,
    ).astype(jnp.bfloat16)
    kv_state = jnp.concatenate([kv_cache[:settled, 0], moved[:, :cache_len]], axis=0)
    conv_state = jnp.concatenate(
        [conv_cache[:settled], moved[:, cache_len:].reshape(moving, conv_len, local_width)], axis=0
    )
    memory = jnp.concatenate([kv_state, fresh], axis=1)
    keys_total = memory.shape[1]
    scores = jnp.einsum(
        "sqd,skd->sqk", queries, memory[..., :head_dim], preferred_element_type=jnp.float32
    ) * head_dim ** (-0.5)
    frame_index = jnp.arange(frame_span, dtype=jnp.int32)
    block_of = frame_index // horizon
    low = block_of * horizon
    high = cache_len + jnp.minimum(frames[:, None], (block_of[None, :] + 1) * horizon)
    position = jnp.arange(keys_total, dtype=jnp.int32)
    live_keys = (position[None, None, :] >= low[None, :, None]) & (
        position[None, None, :] < high[:, :, None]
    )
    scores = jnp.where(live_keys, scores, -1e30)
    row_max = jnp.max(scores, axis=-1, keepdims=True)
    weights = jnp.exp(scores - row_max)
    probabilities = (weights / jnp.sum(weights, axis=-1, keepdims=True)).astype(jnp.bfloat16)
    context = jnp.einsum(
        "sqk,skd->sqd", probabilities, memory[..., head_dim:], preferred_element_type=jnp.float32
    ).astype(jnp.bfloat16)
    ctx_all = lax.all_gather(context, "ingest", axis=0, tiled=False)
    row_count = utterances * frame_span
    attn = jnp.einsum(
        "grc,gcn->rn",
        ctx_all.reshape(groups, row_count, head_dim),
        w_out_full.reshape(groups, head_dim, model_width),
        preferred_element_type=jnp.float32,
    )
    residual = x_plain.reshape(row_count, model_width).astype(jnp.float32) + attn
    normed2 = normalize(residual, ln2_gain)
    mixed = jnp.dot(
        normed2, w_pw1.reshape(model_width, 2 * local_width), preferred_element_type=jnp.float32
    )
    glu_out = (mixed[:, :local_width] * jax.nn.sigmoid(mixed[:, local_width:])).astype(jnp.bfloat16)
    glu_out = glu_out.reshape(utterances, frame_span, local_width)
    joined = jnp.concatenate([conv_state, glu_out], axis=1)
    joined_f = joined.astype(jnp.float32)
    running = jnp.zeros((utterances, frame_span, local_width), jnp.float32)
    for tap_index in range(taps):
        running = running + joined_f[:, tap_index : tap_index + frame_span, :] * dw_weight[
            tap_index
        ].astype(jnp.float32)
    activated = jax.nn.silu(running * bn_scale + bn_shift).astype(jnp.bfloat16)
    act_all = lax.all_gather(activated, "ingest", axis=0, tiled=False)
    conv_terms = jnp.einsum(
        "grc,gcn->rn",
        act_all.reshape(groups, row_count, local_width),
        w_pw2_cols,
        preferred_element_type=jnp.float32,
    )
    residual_own = lax.dynamic_slice_in_dim(residual, me * local_width, local_width, 1)
    result = (residual_own + conv_terms).reshape(utterances, frame_span, local_width)
    live_rows = frame_index[None, :] < frames[:, None]
    layer_out = jnp.where(live_rows[:, :, None], result, 0.0).astype(jnp.bfloat16)
    layer_out = layer_out[:, :out_span]
    keep = jnp.arange(cache_len, dtype=jnp.int32)
    kv_pick = position[None, None, :] == keep[None, :, None] + frames[:, None, None]
    kv_next = jnp.einsum(
        "srp,spd->srd", kv_pick.astype(jnp.bfloat16), memory, preferred_element_type=jnp.float32
    ).astype(jnp.bfloat16)
    conv_keep = jnp.arange(conv_len, dtype=jnp.int32)
    conv_pos = jnp.arange(joined.shape[1], dtype=jnp.int32)
    conv_pick = conv_pos[None, None, :] == conv_keep[None, :, None] + frames[:, None, None]
    conv_next = jnp.einsum(
        "srp,spd->srd", conv_pick.astype(jnp.bfloat16), joined, preferred_element_type=jnp.float32
    ).astype(jnp.bfloat16)
    return (layer_out, kv_next.reshape(kv_cache.shape), conv_next)


def solution(mesh):
    in_specs = (
        P("owner", None, "ingest"),
        P("owner"),
        P("owner"),
        P("owner"),
        P("owner", "ingest", None, None),
        P("owner", None, "ingest"),
        P("owner"),
        P(),
        P(None, "ingest", None),
        P("ingest", None),
        P(),
        P(None, None, "ingest"),
        P(None, "ingest"),
        P("ingest"),
        P("ingest"),
        P("ingest", None),
    )
    out_specs = (
        P("owner", None, "ingest"),
        P("owner", "ingest", None, None),
        P("owner", None, "ingest"),
    )
    return jax.shard_map(shards, mesh=mesh, in_specs=in_specs, out_specs=out_specs, check_vma=False)
```

profile of v0, /device:TPU:1, one launch (start us, length us, event | category | flops | bytes accessed | tf_op | source)
XLA Modules:
  0.0 287.9 jit_solution(12827155608465658466)
XLA Ops:
  10.2 1.1 copy.53
  11.4 19.1 %all-to-all-start = ((bf16[64,32,128]{2,1,0:T(8,128)(2,1)}), bf16[64,32,128]{2,1,0:T(8,128)(2,1)S(1)}, u32[]{:S(2)}, u32[]{:S(2)}) async-start(bf16[64,32,128]{2,1,0:T(8,128)(2,1)} %copy.53), calls=%async_computation | async-start | bytes 1048576 | tf_op jit(solution)/shard_map/all_to_all | solution.py:66
  30.5 29.3 %all-to-all-done = bf16[64,32,128]{2,1,0:T(8,128)(2,1)S(1)} async-done(((bf16[64,32,128]{2,1,0:T(8,128)(2,1)}), bf16[64,32,128]{2,1,0:T(8,128)(2,1)S(1)}, u32[]{:S(2)}, u32[]{:S(2)}) %all-to-all-start) | async-done | bytes 524320 | tf_op jit(solution)/shard_map/all_to_all | solution.py:66
  59.9 1.2 fusion.73
  64.1 3.0 %copy.60 = bf16[64,80,256]{2,1,0:T(8,128)(2,1)} copy(bf16[64,80,256]{2,0,1:T(8,128)(2,1)S(1)} %convolution_convert_fusion) | data formatting | bytes 5242880 | tf_op jit(solution)/shard_map/convert_element_type | solution.py:89
  67.1 8.8 %all-to-all-start.1 = ((bf16[64,80,256]{2,1,0:T(8,128)(2,1)}), bf16[64,80,256]{2,1,0:T(8,128)(2,1)S(1)}, u32[]{:S(2)}, u32[]{:S(2)}) async-start(bf16[64,80,256]{2,1,0:T(8,128)(2,1)} %copy.60), calls=%async_computation.1 | async-start | bytes 5242880 | tf_op jit(solution)/shard_map/all_to_all | solution.py:90
  76.0 15.2 %all-gather.13.cloned.1.call-done = bf16[264,32,128]{2,1,0:T(8,128)(2,1)} async-done(((bf16[33,32,128]{2,1,0:T(8,128)(2,1)}), bf16[264,32,128]{2,1,0:T(8,128)(2,1)}) %all-gather.13.cloned.1.call-update) | async-done | bytes 2162704 | tf_op jit(solution)/shard_map/all_gather | solution.py:102
  93.3 2.5 convert_reduce_fusion
  95.9 1.4 fusion.27
  98.9 1.7 copy_bitcast_fusion
  100.5 26.3 %all-gather.9.cloned.1.call-done = bf16[1024,1024]{1,0:T(8,128)(2,1)} async-done(((bf16[128,1024]{1,0:T(8,128)(2,1)}), bf16[1024,1024]{1,0:T(8,128)(2,1)}) %all-gather.9.cloned.1.call-update) | async-done | bytes 2097168 | tf_op jit(solution)/shard_map/all_gather | solution.py:104
  126.8 35.4 %all-gather.11.cloned.1.call-done = bf16[1024,1024]{1,0:T(8,128)(2,1)} async-done(((bf16[128,1024]{1,0:T(8,128)(2,1)}), bf16[1024,1024]{1,0:T(8,128)(2,1)}) %all-gather.11.cloned.1.call-update) | async-done | bytes 2097168 | tf_op jit(solution)/shard_map/all_gather | solution.py:105
  162.2 2.2 copy.63
  164.4 25.6 %all-to-all-done.1 = bf16[64,80,256]{2,1,0:T(8,128)(2,1)S(1)} async-done(((bf16[64,80,256]{2,1,0:T(8,128)(2,1)}), bf16[64,80,256]{2,1,0:T(8,128)(2,1)S(1)}, u32[]{:S(2)}, u32[]{:S(2)}) %all-to-all-start.1) | async-done | bytes 2621472 | tf_op jit(solution)/shard_map/all_to_all | solution.py:90
  190.1 1.2 fusion.72
  194.0 1.3 fusion.94
  196.9 3.8 %convolution_convert_fusion.3 = bf16[33,32,128]{2,1,0:T(8,128)(2,1)} fusion(bf16[33,102,128]{2,0,1:T(8,128)(2,1)} %get-tuple-element.36, f32[33,32]{1,0:T(8,128)} %fusion.95, f32[33,32,102]{2,1,0:T(8,128)S(1)} %fusion.38), kind=kOutput, calls=%fused_computation.45 | convolution fusion | flops 28033732 | bytes 1567104 | tf_op jit(solution)/shard_map/sqk,skd->sqd/dot_general | solution.py:148
  202.2 32.3 %all-gather.15.cloned.1.call-done = bf16[264,32,128]{2,1,0:T(8,128)(2,1)} async-done(((bf16[33,32,128]{2,1,0:T(8,128)(2,1)}), bf16[264,32,128]{2,1,0:T(8,128)(2,1)}) %all-gather.15.cloned.1.call-update) | async-done | bytes 2162704 | tf_op jit(solution)/shard_map/all_gather | solution.py:151
  234.5 5.7 %fusion.93 = (f32[1056]{0:T(1024)S(1)}, f32[1056]{0:T(1024)S(1)}, f32[1056,1024]{1,0:T(8,128)S(1)}) fusion(bf16[8,1056,128]{2,1,0:T(8,128)(2,1)} %bitcast.116, bf16[8,128,1024]{2,1,0:T(8,128)(2,1)} %bitcast.117, bf16[1056,1024]{1,0:T(8,128)(2,1)} %bitcast.109), kind=kOutput, calls=%fused_computation.149 | convolution fusion | flops 2219997184 | bytes 10756352 | tf_op jit(solution)/shard_map/grc,gcn->rn/dot_general | solution.py:153
  241.0 1.2 copy-done.2
  242.9 1.4 multiply_convert_fusion.2
  245.5 2.0 fusion.24
  248.4 29.6 %all-gather.17.cloned.1.call-done = bf16[264,32,128]{2,1,0:T(8,128)(2,1)} async-done(((bf16[33,32,128]{2,1,0:T(8,128)(2,1)}), bf16[264,32,128]{2,1,0:T(8,128)(2,1)}) %all-gather.17.cloned.1.call-update) | async-done | bytes 2162704 | tf_op jit(solution)/shard_map/all_gather | solution.py:174
  278.0 2.4 fusion.5
  (91 shorter events, 19.9 us)
Async XLA Ops:
  7.2 88.7 %copy-start = (bf16[1024,1,384]{2,0,1:T(8,128)(2,1)S(1)}, bf16[1024,1,384]{2,0,1:T(8,128)(2,1)}, u32[]{:S(2)}) copy-start(bf16[1024,1,384]{2,0,1:T(8,128)(2,1)} %param.24) | copy-start | bytes 2359300
  10.2 52.1 %slice-start.2 = ((bf16[33,8,128]{2,1,0:T(8,128)(2,1)}), bf16[32,8,128]{2,1,0:T(8,128)(2,1)S(1)}, s32[]{:S(2)}) async-start(bf16[33,8,128]{2,1,0:T(8,128)(2,1)} %param.21), calls=%async_computation.9 | async-start | bytes 131072 | tf_op jit(solution)/shard_map/slice | solution.py:78
  11.4 48.5 %all-to-all-start = ((bf16[64,32,128]{2,1,0:T(8,128)(2,1)}), bf16[64,32,128]{2,1,0:T(8,128)(2,1)S(1)}, u32[]{:S(2)}, u32[]{:S(2)}) async-start(bf16[64,32,128]{2,1,0:T(8,128)(2,1)} %copy.53), calls=%async_computation | async-start | bytes 1048576 | tf_op jit(solution)/shard_map/all_to_all | solution.py:66
  30.5 60.7 %all-gather.13.cloned.1.call-start = ((), (), s32[]{:S(2)}) async-start(), calls=%async_computation.4 | async-start | bytes 2433024 | tf_op jit(solution)/shard_map/all_gather | solution.py:102
  61.4 1.4 slice-start.1
  62.4 0.7 copy-start.11
  67.1 26.1 %copy-start.8 = (s32[33]{0:T(128)S(1)}, s32[33]{0:T(128)}, u32[]{:S(2)}) copy-start(s32[33]{0:T(128)} %param.19) | copy-start | bytes 400
  67.1 122.9 %all-to-all-start.1 = ((bf16[64,80,256]{2,1,0:T(8,128)(2,1)}), bf16[64,80,256]{2,1,0:T(8,128)(2,1)S(1)}, u32[]{:S(2)}, u32[]{:S(2)}) async-start(bf16[64,80,256]{2,1,0:T(8,128)(2,1)} %copy.60), calls=%async_computation.1 | async-start | bytes 5242880 | tf_op jit(solution)/shard_map/all_to_all | solution.py:90
  75.9 19.9 %copy-start.14 = (f32[1024]{0:T(1024)S(1)}, f32[1024]{0:T(1024)}, u32[]{:S(2)}) copy-start(f32[1024]{0:T(1024)} %param.23) | copy-start | bytes 12292
  75.9 50.9 %all-gather.9.cloned.1.call-start = ((), (), s32[]{:S(2)}) async-start(), calls=%async_computation.2 | async-start | bytes 2359296 | tf_op jit(solution)/shard_map/all_gather | solution.py:104
  91.2 71.0 %all-gather.11.cloned.1.call-start = ((), (), s32[]{:S(2)}) async-start(), calls=%async_computation.3 | async-start | bytes 2359296 | tf_op jit(solution)/shard_map/all_gather | solution.py:105
  91.9 142.5 %all-gather.15.cloned.1.call-start = ((), (), s32[]{:S(2)}) async-start(), calls=%async_computation.5 | async-start | bytes 2433024 | tf_op jit(solution)/shard_map/all_gather | solution.py:151
  92.2 3.7 %copy-start.1 = (bf16[264,32,128]{2,1,0:T(8,128)(2,1)S(1)}, bf16[264,32,128]{2,1,0:T(8,128)(2,1)}, u32[]{:S(2)}) copy-start(bf16[264,32,128]{2,1,0:T(8,128)(2,1)} %all-gather.13.cloned.1.call-done) | copy-start | bytes 6488068
  191.3 1.9 copy-start.4
  192.1 1.0 copy-start.3
  194.0 1.3 copy-start.6
  196.0 5.1 %copy-start.7 = (bf16[33,8,128]{2,1,0:T(8,128)(2,1)S(1)}, bf16[33,8,128]{2,1,0:T(8,128)(2,1)}, u32[]{:S(2)}) copy-start(bf16[33,8,128]{2,1,0:T(8,128)(2,1)} %param.21) | copy-start | bytes 202756
  196.0 6.1 %slice-start = ((bf16[32,74,256]{2,0,1:T(8,128)(2,1)}), bf16[32,4,256]{2,0,1:T(8,128)(2,1)S(1)}, s32[]{:S(2)}) async-start(bf16[32,74,256]{2,0,1:T(8,128)(2,1)} %copy-done.3), calls=%async_computation.7 | async-start | bytes 131072 | tf_op jit(solution)/shard_map/slice | solution.py:129
  200.8 77.2 %all-gather.17.cloned.1.call-start = ((), (), s32[]{:S(2)}) async-start(), calls=%async_computation.6 | async-start | bytes 2433024 | tf_op jit(solution)/shard_map/all_gather | solution.py:174
  234.5 5.7 %copy-start.5 = (bf16[1024,2,128]{2,1,0:T(2,128)(2,1)S(1)}, bf16[1024,2,128]{2,1,0:T(2,128)(2,1)}, u32[]{:S(2)}) copy-start(bf16[1024,2,128]{2,1,0:T(2,128)(2,1)} %param.27) | copy-start | bytes 1572868
  234.5 5.7 %copy-start.10 = (f32[1024]{0:T(1024)S(1)}, f32[1024]{0:T(1024)}, u32[]{:S(2)}) copy-start(f32[1024]{0:T(1024)} %param.26) | copy-start | bytes 12292
  240.1 2.1 copy-start.2
  242.2 0.7 copy-start.13
  242.9 1.4 copy-start.9
  (1 other events, 0.7 us)
Sparse Core Ops, SparseCore 0:
  62.4 28.7 all-gather.12
  93.3 33.4 all-gather.8
  129.0 33.2 all-gather.10
  200.9 33.4 all-gather.14
  244.4 33.5 all-gather.16
where the time goes:
time: 288 us
  waiting for transfers between devices  195 us (68%)
  starting transfers between devices  28.5 us (10%)
  matrix products  20.8 us (7%)
  local copies, waits for them, and re-layouts  18.7 us (6%)
  between operations  14.1 us (5%)
  other arithmetic  11.3 us (4%)
    all_gather x1, waiting for transfers between devices, shards(): w_pw2_full = lax.all_gather(w_pw2_in, 'ingest', axis=0, tiled=True)  35.4 us
    all_gather x1, waiting for transfers between devices, shards(): ctx_all = lax.all_gather(context, 'ingest', axis=0, tiled=False)  32.3 us
    all_gather x1, waiting for transfers between devices, shards(): act_all = lax.all_gather(activated, 'ingest', axis=0, tiled=False)  29.6 us
    all_to_all x1, waiting for transfers between devices, shards(): lax.all_to_all(frame_send, 'owner', split_axis=0, concat_axis=0, tiled=True)  29.3 us
    all_gather x1, waiting for transfers between devices, shards(): w_out_full = lax.all_gather(w_out_in, 'ingest', axis=0, tiled=True)  26.3 us
    all_to_all x1, waiting for transfers between devices, shards(): lax.all_to_all(cache_send, 'owner', split_axis=0, concat_axis=0, tiled=True)  25.6 us
    all_to_all x1, starting transfers between devices, shards(): lax.all_to_all(frame_send, 'owner', split_axis=0, concat_axis=0, tiled=True)  19.1 us
    all_gather x1, waiting for transfers between devices, shards(): x_all = lax.all_gather(arranged, 'ingest', axis=0, tiled=False)  15.2 us
  transfers between devices with their start and end apart: 7, of which 7 were waited for; matrix products, arithmetic and copies ran while one was open for 7% of the time, Pallas kernels for 0%

commit v1 on v0

--- a/solution.py
+++ b/solution.py
@@ -102,7 +102,14 @@
     x_all = lax.all_gather(arranged, "ingest", axis=0, tiled=False)
     w_out_in, w_pw2_in, x_all = lax.optimization_barrier((w_out, w_pw2, x_all))
     w_out_full = lax.all_gather(w_out_in, "ingest", axis=0, tiled=True)
-    w_pw2_full = lax.all_gather(w_pw2_in, "ingest", axis=0, tiled=True)
+    ring = [w_pw2_in]
+    for hop in range(7):
+        ring.append(lax.ppermute(ring[-1], "ingest", [(dev, (dev + 1) % 8) for dev in range(8)]))
+    w_pw2_full = jnp.roll(
+        jnp.concatenate(ring[::-1], axis=0),
+        (lax.axis_index("ingest") + 1) * ring[0].shape[0],
+        axis=0,
+    )
     x_plain = x_all.transpose(1, 2, 0, 3).reshape(utterances, frame_span, model_width)
     normed = normalize(x_plain.astype(jnp.float32), ln1_gain)
     projected = jnp.dot(

time: 288 us -> 281 us (0.976)
  waiting for transfers between devices: 195 us -> 167 us
  starting transfers between devices: 28.5 us -> 36.8 us
  local copies, waits for them, and re-layouts: 18.7 us -> 26 us
  matrix products: 20.8 us -> 23.7 us
    all_gather x1 -> x0, waiting for transfers between devices: 35.4 us -> none  [shards(): w_pw2_full = lax.all_gather(w_pw2_in, 'ingest', axis=0, tiled=True)]
    ppermute x0 -> x7, waiting for transfers between devices: none -> 31.2 us  [shards(): lax.ppermute(ring[-1], 'ingest', [(dev, (dev + 1) % 8) for dev in range(8)])]
    all_gather x1, waiting for transfers between devices: 26.3 us -> 0.01 us  [shards(): w_out_full = lax.all_gather(w_out_in, 'ingest', axis=0, tiled=True)]
    all_gather x1, waiting for transfers between devices: 15.2 us -> 35.3 us  [shards(): x_all = lax.all_gather(arranged, 'ingest', axis=0, tiled=False)]
    all_to_all x1, waiting for transfers between devices: 25.6 us -> 14.1 us  [shards(): lax.all_to_all(cache_send, 'owner', split_axis=0, concat_axis=0, tiled=True)]
    ppermute x0 -> x7, starting transfers between devices: none -> 8.24 us  [shards(): lax.ppermute(ring[-1], 'ingest', [(dev, (dev + 1) % 8) for dev in range(8)])]
    unnamed x33 -> x56, local copies, waits for them, and re-layouts: 4.08 us -> 10.3 us
    all_to_all x1, waiting for transfers between devices: 29.3 us -> 24.2 us  [shards(): lax.all_to_all(frame_send, 'owner', split_axis=0, concat_axis=0, tiled=True)]
  transfers between devices with their start and end apart: 7 -> 13, of which waited for: 7 -> 12; matrix products, arithmetic and copies ran while one was open for 7% -> 12% of each run, Pallas kernels for 0% -> 0%
where the time goes in v1:
time: 281 us; the launch traced here: 280 us
  waiting for transfers between devices  167 us (59%)
  starting transfers between devices  36.8 us (13%)
  local copies, waits for them, and re-layouts  26 us (9%)
  matrix products  23.7 us (8%)
  between operations  14.3 us (5%)
  other arithmetic  12.7 us (5%)
    all_gather x1, waiting for transfers between devices, shards(): x_all = lax.all_gather(arranged, 'ingest', axis=0, tiled=False)  35.3 us
    all_gather x1, waiting for transfers between devices, shards(): ctx_all = lax.all_gather(context, 'ingest', axis=0, tiled=False)  32.3 us
    ppermute x7, waiting for transfers between devices, shards(): lax.ppermute(ring[-1], 'ingest', [(dev, (dev + 1) % 8) for dev in range(8)])  31.2 us
    all_gather x1, waiting for transfers between devices, shards(): act_all = lax.all_gather(activated, 'ingest', axis=0, tiled=False)  29.6 us
    all_to_all x1, waiting for transfers between devices, shards(): lax.all_to_all(frame_send, 'owner', split_axis=0, concat_axis=0, tiled=True)  24.2 us
    all_to_all x1, starting transfers between devices, shards(): lax.all_to_all(frame_send, 'owner', split_axis=0, concat_axis=0, tiled=True)  19.4 us
    all_to_all x1, waiting for transfers between devices, shards(): lax.all_to_all(cache_send, 'owner', split_axis=0, concat_axis=0, tiled=True)  14.1 us
    unnamed x56, local copies, waits for them, and re-layouts  10.3 us
  transfers between devices with their start and end apart: 13, of which 12 were waited for; matrix products, arithmetic and copies ran while one was open for 12% of the time, Pallas kernels for 0%

profile of v1, /device:TPU:1, one launch (start us, length us, event | category | flops | bytes accessed | tf_op | source)
XLA Modules:
  0.0 280.2 jit_solution(17933945551732412537)
XLA Ops:
  11.4 19.4 %all-to-all-start = ((bf16[64,32,128]{2,1,0:T(8,128)(2,1)}), bf16[64,32,128]{2,1,0:T(8,128)(2,1)}, u32[]{:S(2)}, u32[]{:S(2)}) async-start(bf16[64,32,128]{2,1,0:T(8,128)(2,1)} %copy.53), calls=%async_computation | async-start | bytes 1048576 | tf_op jit(solution)/shard_map/all_to_all | solution.py:66
  32.9 3.0 %copy.60 = bf16[64,80,256]{2,1,0:T(8,128)(2,1)} copy(bf16[64,80,256]{2,0,1:T(8,128)(2,1)S(1)} %convolution_convert_fusion) | data formatting | bytes 5242880 | tf_op jit(solution)/shard_map/convert_element_type | solution.py:89
  35.9 24.2 %all-to-all-done = bf16[64,32,128]{2,1,0:T(8,128)(2,1)} async-done(((bf16[64,32,128]{2,1,0:T(8,128)(2,1)}), bf16[64,32,128]{2,1,0:T(8,128)(2,1)}, u32[]{:S(2)}, u32[]{:S(2)}) %all-to-all-start) | async-done | bytes 524320 | tf_op jit(solution)/shard_map/all_to_all | solution.py:66
  60.1 8.7 %all-to-all-start.1 = ((bf16[64,80,256]{2,1,0:T(8,128)(2,1)}), bf16[64,80,256]{2,1,0:T(8,128)(2,1)S(1)}, u32[]{:S(2)}, u32[]{:S(2)}) async-start(bf16[64,80,256]{2,1,0:T(8,128)(2,1)} %copy.60), calls=%async_computation.1 | async-start | bytes 5242880 | tf_op jit(solution)/shard_map/all_to_all | solution.py:90
  73.1 35.3 %all-gather.10.cloned.1.call-done = bf16[264,32,128]{2,1,0:T(8,128)(2,1)} async-done(((bf16[33,32,128]{2,1,0:T(8,128)(2,1)}), bf16[264,32,128]{2,1,0:T(8,128)(2,1)}) %all-gather.10.cloned.1.call-update) | async-done | bytes 2162704 | tf_op jit(solution)/shard_map/all_gather | solution.py:102
  108.6 3.6 %collective-permute-done = bf16[128,1024]{1,0:T(8,128)(2,1)S(1)} collective-permute-done((bf16[128,1024]{1,0:T(8,128)(2,1)}, bf16[128,1024]{1,0:T(8,128)(2,1)S(1)}, u32[]{:S(2)}, u32[]{:S(2)}) %collective-permute-start) | collective-permute-done | bytes 262176 | tf_op jit(solution)/shard_map/ppermute | solution.py:107
  112.9 2.4 collective-permute-start.1
  116.1 2.5 collective-permute-done.1
  118.6 2.6 collective-permute-start.2
  121.6 3.6 %collective-permute-done.2 = bf16[128,1024]{1,0:T(8,128)(2,1)} collective-permute-done((bf16[128,1024]{1,0:T(8,128)(2,1)}, bf16[128,1024]{1,0:T(8,128)(2,1)}, u32[]{:S(2)}, u32[]{:S(2)}) %collective-permute-start.2) | collective-permute-done | bytes 262176 | tf_op jit(solution)/shard_map/ppermute | solution.py:107
  125.1 2.2 collective-permute-start.3
  128.1 4.4 %collective-permute-done.3 = bf16[128,1024]{1,0:T(8,128)(2,1)} collective-permute-done((bf16[128,1024]{1,0:T(8,128)(2,1)}, bf16[128,1024]{1,0:T(8,128)(2,1)}, u32[]{:S(2)}, u32[]{:S(2)}) %collective-permute-start.3) | collective-permute-done | bytes 262176 | tf_op jit(solution)/shard_map/ppermute | solution.py:107
  133.4 2.4 convert_reduce_fusion
  135.9 3.8 %collective-permute-done.4 = bf16[128,1024]{1,0:T(8,128)(2,1)S(1)} collective-permute-done((bf16[128,1024]{1,0:T(8,128)(2,1)}, bf16[128,1024]{1,0:T(8,128)(2,1)S(1)}, u32[]{:S(2)}, u32[]{:S(2)}) %collective-permute-start.4) | collective-permute-done | bytes 262176 | tf_op jit(solution)/shard_map/ppermute | solution.py:107
  139.7 3.2 %fusion.27 = bf16[33,32,384]{2,1,0:T(8,128)(2,1)S(1)} fusion(bf16[1024,1,384]{2,0,1:T(8,128)(2,1)S(1)} %copy-done, bf16[8,33,32,128]{3,2,1,0:T(8,128)(2,1)} %bitcast.104, f32[8,128]{1,0:T(8,128)S(1)} %bitcast.117, f32[33,32]{1,0:T(8,128)S(1)} %get-tuple-element.38, f32[33,32]{1,0:T(8,128)S(1)} %get-tuple-element.37), kind=kOutput, calls=%fused_computation.31 | convolution fusion | flops 836284416 | bytes 3772672 | tf_op jit(solution)/shard_map/dot_general | solution.py:115
  143.9 2.8 %collective-permute-done.5 = bf16[128,1024]{1,0:T(8,128)(2,1)S(1)} collective-permute-done((bf16[128,1024]{1,0:T(8,128)(2,1)S(1)}, bf16[128,1024]{1,0:T(8,128)(2,1)S(1)}, u32[]{:S(2)}, u32[]{:S(2)}) %collective-permute-start.5) | collective-permute-done | bytes 262176 | tf_op jit(solution)/shard_map/ppermute | solution.py:107
  148.4 10.5 %collective-permute-done.6 = bf16[128,1024]{1,0:T(8,128)(2,1)S(1)} collective-permute-done((bf16[128,1024]{1,0:T(8,128)(2,1)S(1)}, bf16[128,1024]{1,0:T(8,128)(2,1)S(1)}, u32[]{:S(2)}, u32[]{:S(2)}) %collective-permute-start.6) | collective-permute-done | bytes 262176 | tf_op jit(solution)/shard_map/ppermute | solution.py:107
  166.5 2.2 copy.63
  168.7 14.1 %all-to-all-done.1 = bf16[64,80,256]{2,1,0:T(8,128)(2,1)S(1)} async-done(((bf16[64,80,256]{2,1,0:T(8,128)(2,1)}), bf16[64,80,256]{2,1,0:T(8,128)(2,1)S(1)}, u32[]{:S(2)}, u32[]{:S(2)}) %all-to-all-start.1) | async-done | bytes 2621472 | tf_op jit(solution)/shard_map/all_to_all | solution.py:90
  189.8 3.8 %convolution_convert_fusion.3 = bf16[33,32,128]{2,1,0:T(8,128)(2,1)} fusion(bf16[33,102,128]{2,0,1:T(8,128)(2,1)} %get-tuple-element.36, f32[33,32]{1,0:T(8,128)} %fusion.95, f32[33,32,102]{2,1,0:T(8,128)S(1)} %fusion.38), kind=kOutput, calls=%fused_computation.45 | convolution fusion | flops 28033732 | bytes 1567104 | tf_op jit(solution)/shard_map/sqk,skd->sqd/dot_general | solution.py:155
  195.0 32.3 %all-gather.12.cloned.1.call-done = bf16[264,32,128]{2,1,0:T(8,128)(2,1)} async-done(((bf16[33,32,128]{2,1,0:T(8,128)(2,1)}), bf16[264,32,128]{2,1,0:T(8,128)(2,1)}) %all-gather.12.cloned.1.call-update) | async-done | bytes 2162704 | tf_op jit(solution)/shard_map/all_gather | solution.py:158
  227.3 5.7 %fusion.93 = (f32[1056]{0:T(1024)S(1)}, f32[1056]{0:T(1024)S(1)}, f32[1056,1024]{1,0:T(8,128)S(1)}) fusion(bf16[8,1056,128]{2,1,0:T(8,128)(2,1)} %bitcast.115, bf16[8,128,1024]{2,1,0:T(8,128)(2,1)} %bitcast.116, bf16[1056,1024]{1,0:T(8,128)(2,1)} %bitcast.109), kind=kOutput, calls=%fused_computation.166 | convolution fusion | flops 2219997184 | bytes 10756352 | tf_op jit(solution)/shard_map/grc,gcn->rn/dot_general | solution.py:160
  240.8 29.6 %all-gather.14.cloned.1.call-done = bf16[264,32,128]{2,1,0:T(8,128)(2,1)} async-done(((bf16[33,32,128]{2,1,0:T(8,128)(2,1)}), bf16[264,32,128]{2,1,0:T(8,128)(2,1)}) %all-gather.14.cloned.1.call-update) | async-done | bytes 2162704 | tf_op jit(solution)/shard_map/all_gather | solution.py:181
  270.4 2.4 fusion.5
  (128 shorter events, 41.4 us)
Async XLA Ops:
  7.2 132.5 %copy-start = (bf16[1024,1,384]{2,0,1:T(8,128)(2,1)S(1)}, bf16[1024,1,384]{2,0,1:T(8,128)(2,1)}, u32[]{:S(2)}) copy-start(bf16[1024,1,384]{2,0,1:T(8,128)(2,1)} %param.24) | copy-start | bytes 2359300
  9.1 21.7 %slice-start.1 = ((bf16[33,1,70,256]{3,2,1,0:T(8,128)(2,1)}), bf16[32,1,70,256]{3,2,1,0:T(8,128)(2,1)S(1)}, s32[]{:S(2)}) async-start(bf16[33,1,70,256]{3,2,1,0:T(8,128)(2,1)} %param.20), calls=%async_computation.7 | async-start | bytes 2359296 | tf_op jit(solution)/shard_map/slice | solution.py:77
  11.4 48.6 %all-to-all-start = ((bf16[64,32,128]{2,1,0:T(8,128)(2,1)}), bf16[64,32,128]{2,1,0:T(8,128)(2,1)}, u32[]{:S(2)}, u32[]{:S(2)}) async-start(bf16[64,32,128]{2,1,0:T(8,128)(2,1)} %copy.53), calls=%async_computation | async-start | bytes 1048576 | tf_op jit(solution)/shard_map/all_to_all | solution.py:66
  60.1 122.8 %all-to-all-start.1 = ((bf16[64,80,256]{2,1,0:T(8,128)(2,1)}), bf16[64,80,256]{2,1,0:T(8,128)(2,1)S(1)}, u32[]{:S(2)}, u32[]{:S(2)}) async-start(bf16[64,80,256]{2,1,0:T(8,128)(2,1)} %copy.60), calls=%async_computation.1 | async-start | bytes 5242880 | tf_op jit(solution)/shard_map/all_to_all | solution.py:90
  68.7 58.7 %copy-start.12 = (s32[33]{0:T(128)S(1)}, s32[33]{0:T(128)}, u32[]{:S(2)}) copy-start(s32[33]{0:T(128)} %param.19) | copy-start | bytes 400
  68.7 70.9 %copy-start.18 = (f32[1024]{0:T(1024)S(1)}, f32[1024]{0:T(1024)}, u32[]{:S(2)}) copy-start(f32[1024]{0:T(1024)} %param.23) | copy-start | bytes 12292
  68.7 39.7 %all-gather.10.cloned.1.call-start = ((), (), s32[]{:S(2)}) async-start(), calls=%async_computation.3 | async-start | bytes 2433024 | tf_op jit(solution)/shard_map/all_gather | solution.py:102
  73.1 93.4 %all-gather.8.cloned.1.call-start = ((), (), s32[]{:S(2)}) async-start(), calls=%async_computation.2 | async-start | bytes 2359296 | tf_op jit(solution)/shard_map/all_gather | solution.py:104
  108.5 3.8 %collective-permute-start = (bf16[128,1024]{1,0:T(8,128)(2,1)}, bf16[128,1024]{1,0:T(8,128)(2,1)S(1)}, u32[]{:S(2)}, u32[]{:S(2)}) collective-permute-start(bf16[128,1024]{1,0:T(8,128)(2,1)} %param.31), channel_id=1, source_target_pairs={{0,64},{64,128},{128,192},{192,256},{256,320},{320,384},{384,448},... | collective-permute-start | bytes 786440 | tf_op jit(solution)/shard_map/ppermute | solution.py:107
  112.9 5.7 %collective-permute-start.1 = (bf16[128,1024]{1,0:T(8,128)(2,1)S(1)}, bf16[128,1024]{1,0:T(8,128)(2,1)}, u32[]{:S(2)}, u32[]{:S(2)}) collective-permute-start(bf16[128,1024]{1,0:T(8,128)(2,1)S(1)} %collective-permute-done), channel_id=1, source_target_pairs={{0,64},{64,128},{128,192},{192,256},{256,320},{320,384},{384,448},... | collective-permute-start | bytes 786440 | tf_op jit(solution)/shard_map/ppermute | solution.py:107
  118.6 6.5 %collective-permute-start.2 = (bf16[128,1024]{1,0:T(8,128)(2,1)}, bf16[128,1024]{1,0:T(8,128)(2,1)}, u32[]{:S(2)}, u32[]{:S(2)}) collective-permute-start(bf16[128,1024]{1,0:T(8,128)(2,1)} %collective-permute-done.1), channel_id=1, source_target_pairs={{0,64},{64,128},{128,192},{192,256},{256,320},{320,384},{384,448},... | collective-permute-start | bytes 786440 | tf_op jit(solution)/shard_map/ppermute | solution.py:107
  121.2 106.0 %all-gather.12.cloned.1.call-start = ((), (), s32[]{:S(2)}) async-start(), calls=%async_computation.4 | async-start | bytes 2433024 | tf_op jit(solution)/shard_map/all_gather | solution.py:158
  125.1 7.3 %collective-permute-start.3 = (bf16[128,1024]{1,0:T(8,128)(2,1)}, bf16[128,1024]{1,0:T(8,128)(2,1)}, u32[]{:S(2)}, u32[]{:S(2)}) collective-permute-start(bf16[128,1024]{1,0:T(8,128)(2,1)} %collective-permute-done.2), channel_id=1, source_target_pairs={{0,64},{64,128},{128,192},{192,256},{256,320},{320,384},{384,448},... | collective-permute-start | bytes 786440 | tf_op jit(solution)/shard_map/ppermute | solution.py:107
  132.5 7.2 %collective-permute-start.4 = (bf16[128,1024]{1,0:T(8,128)(2,1)}, bf16[128,1024]{1,0:T(8,128)(2,1)S(1)}, u32[]{:S(2)}, u32[]{:S(2)}) collective-permute-start(bf16[128,1024]{1,0:T(8,128)(2,1)} %collective-permute-done.3), channel_id=1, source_target_pairs={{0,64},{64,128},{128,192},{192,256},{256,320},{320,384},{384,448},... | collective-permute-start | bytes 786440 | tf_op jit(solution)/shard_map/ppermute | solution.py:107
  139.7 7.0 %collective-permute-start.5 = (bf16[128,1024]{1,0:T(8,128)(2,1)S(1)}, bf16[128,1024]{1,0:T(8,128)(2,1)S(1)}, u32[]{:S(2)}, u32[]{:S(2)}) collective-permute-start(bf16[128,1024]{1,0:T(8,128)(2,1)S(1)} %collective-permute-done.4), channel_id=1, source_target_pairs={{0,64},{64,128},{128,192},{192,256},{256,320},{320,384},{384,448},... | collective-permute-start | bytes 786440 | tf_op jit(solution)/shard_map/ppermute | solution.py:107
  139.7 7.0 %copy-start.1 = (bf16[264,32,128]{2,1,0:T(8,128)(2,1)S(1)}, bf16[264,32,128]{2,1,0:T(8,128)(2,1)}, u32[]{:S(2)}) copy-start(bf16[264,32,128]{2,1,0:T(8,128)(2,1)} %all-gather.10.cloned.1.call-done) | copy-start | bytes 6488068
  146.7 12.2 %collective-permute-start.6 = (bf16[128,1024]{1,0:T(8,128)(2,1)S(1)}, bf16[128,1024]{1,0:T(8,128)(2,1)S(1)}, u32[]{:S(2)}, u32[]{:S(2)}) collective-permute-start(bf16[128,1024]{1,0:T(8,128)(2,1)S(1)} %collective-permute-done.5), channel_id=1, source_target_pairs={{0,64},{64,128},{128,192},{192,256},{256,320},{320,384},{384,448},... | collective-permute-start | bytes 786440 | tf_op jit(solution)/shard_map/ppermute | solution.py:107
  148.4 13.5 %copy-start.7 = (bf16[128,1024]{1,0:T(8,128)(2,1)S(1)}, bf16[128,1024]{1,0:T(8,128)(2,1)}, u32[]{:S(2)}) copy-start(bf16[128,1024]{1,0:T(8,128)(2,1)} %copy-done.6) | copy-start | bytes 786436
  148.4 13.5 %copy-start.5 = (bf16[128,1024]{1,0:T(8,128)(2,1)S(1)}, bf16[128,1024]{1,0:T(8,128)(2,1)}, u32[]{:S(2)}) copy-start(bf16[128,1024]{1,0:T(8,128)(2,1)} %param.31) | copy-start | bytes 786436
  188.2 5.7 %copy-start.10 = (bf16[33,8,128]{2,1,0:T(8,128)(2,1)S(1)}, bf16[33,8,128]{2,1,0:T(8,128)(2,1)}, u32[]{:S(2)}) copy-start(bf16[33,8,128]{2,1,0:T(8,128)(2,1)} %param.21) | copy-start | bytes 202756
  188.2 6.7 %slice-start = ((bf16[32,74,256]{2,0,1:T(8,128)(2,1)}), bf16[32,4,256]{2,0,1:T(8,128)(2,1)S(1)}, s32[]{:S(2)}) async-start(bf16[32,74,256]{2,0,1:T(8,128)(2,1)} %copy-done.3), calls=%async_computation.6 | async-start | bytes 131072 | tf_op jit(solution)/shard_map/slice | solution.py:136
  193.6 76.7 %all-gather.14.cloned.1.call-start = ((), (), s32[]{:S(2)}) async-start(), calls=%async_computation.5 | async-start | bytes 2433024 | tf_op jit(solution)/shard_map/all_gather | solution.py:181
  227.3 5.7 %copy-start.9 = (bf16[1024,2,128]{2,1,0:T(2,128)(2,1)S(1)}, bf16[1024,2,128]{2,1,0:T(2,128)(2,1)}, u32[]{:S(2)}) copy-start(bf16[1024,2,128]{2,1,0:T(2,128)(2,1)} %param.27) | copy-start | bytes 1572868
  227.3 5.7 %copy-start.14 = (f32[1024]{0:T(1024)S(1)}, f32[1024]{0:T(1024)}, u32[]{:S(2)}) copy-start(f32[1024]{0:T(1024)} %param.26) | copy-start | bytes 12292
  (12 other events, 20.0 us)
Sparse Core Ops, SparseCore 0:
  73.2 35.2 all-gather.9
  121.4 37.7 all-gather.7
  193.8 33.4 all-gather.11
  236.8 33.5 all-gather.13
